TPU v7x, 32 devices: a whole 2x2x4 slice. The times are simulated.
32 devices in a mesh: groups: 2 (over y), video: 4 (over z), tensor: 4 (over x, core).
Axes of the slice: x: 2, y: 2, z: 4, core: 2. Of those that a mesh axis runs over, the one named last changes fastest.
Arguments:
- frames: bfloat16 [24, 256, 6144], P(('groups', 'video')), parts along dimension 0, may hold values from -610 to 610
- frame_video: int32 [24], P(('groups', 'video')), parts along dimension 0, may hold values from 0 to 3, never falling along the last dimension, each value on 1 to 6 neighbouring positions
- qkv_weight: bfloat16 [6144, 3, 3072], P('video', None, 'tensor'), may hold values from -0.078125 to 0.078125
- conn_weight: bfloat16 [3072, 3, 4096], P('tensor', None, 'video'), may hold values from -6 to 6
Outputs:
- summary: bfloat16 [384, 4096], P(('groups', 'video'), 'tensor'), parts along dimension 0
There are 2 independent parts, one for each index of `groups`. A program takes and returns all parts, laid end to end along the dimension named above; an argument that names none is the same for every part. Nothing has to cross between parts.
All inputs are finite; a program needn't handle non-finite values.
Results may differ from a plain program's by a relative error of at most 0.009.
Values may be sent and summed in bfloat16 or wider, within the bound.
No kernel may reach another device: no remote copies, remote signals or barrier semaphores. Data moves between devices by JAX's collectives and lax.ppermute only.
A program may use at most 192 MiB of HBM per device.

v0:
```python
import math
import jax
import jax.numpy as jnp
from jax import lax
from jax.sharding import PartitionSpec as P

HD = 128
PATCH = 256
POOL = 16


def rms_norm(values):
    return values * lax.rsqrt(jnp.mean(values * values, axis=-1, keepdims=True) + 1e-06)


def per_device(frames, frame_video, qkv_weight, conn_weight):
    scale = 1.0 / math.sqrt(HD)
    blocks = math.isqrt(POOL)
    inner = math.isqrt(PATCH) // blocks
    nframes = frames.shape[0]
    patch_rows = nframes * PATCH
    wide = frames.astype(jnp.float32)
    center = wide - jnp.mean(wide, axis=-1, keepdims=True)
    normed = center * lax.rsqrt(jnp.mean(center * center, axis=-1, keepdims=True) + 1e-06)
    normed = normed.astype(jnp.bfloat16).reshape(patch_rows, frames.shape[2])
    local_cols = qkv_weight.shape[1] * qkv_weight.shape[2]
    piece = lax.all_gather(qkv_weight, "video", axis=0, tiled=True)
    proj = jnp.dot(
        normed, piece.reshape(piece.shape[0], local_cols), preferred_element_type=jnp.float32
    )
    heads_local = qkv_weight.shape[2] // HD
    proj = proj.reshape(nframes, PATCH, 3, heads_local, HD)
    query = rms_norm(proj[:, :, 0]).astype(jnp.bfloat16)
    keys = rms_norm(proj[:, :, 1]).astype(jnp.bfloat16)
    values = proj[:, :, 2].astype(jnp.bfloat16)
    scores = jnp.einsum("fphd,fkhd->fhpk", query, keys, preferred_element_type=jnp.float32) * scale
    probs = jnp.exp(scores)
    probs = (probs / jnp.sum(probs, axis=-1, keepdims=True)).astype(jnp.bfloat16)
    attended = jnp.einsum("fhpk,fkhd->fphd", probs, values, preferred_element_type=jnp.float32)
    grid = attended.reshape(nframes, blocks, inner, blocks, inner, heads_local, HD)
    pooled = (
        jnp.mean(grid, axis=(2, 4)).reshape(nframes * POOL, heads_local * HD).astype(jnp.bfloat16)
    )
    rows = nframes * POOL
    partial_proj = jnp.einsum(
        "rc,ckt->rkt",
        pooled,
        lax.all_gather(conn_weight, "video", axis=2, tiled=True),
        preferred_element_type=jnp.float32,
    )
    clip_proj = lax.psum_scatter(
        partial_proj.astype(jnp.bfloat16), "tensor", scatter_dimension=2, tiled=True
    ).astype(jnp.float32)
    t_heads = clip_proj.shape[2] // HD
    tquery = rms_norm(clip_proj[:, 0].reshape(rows, t_heads, HD)).astype(jnp.bfloat16)
    tkey = rms_norm(clip_proj[:, 1].reshape(rows, t_heads, HD)).astype(jnp.bfloat16)
    tvalue = clip_proj[:, 2].astype(jnp.bfloat16)
    tkey_flat = tkey.reshape(rows, t_heads * HD)
    seg_rows = jnp.repeat(frame_video, POOL)
    query_frame = lax.axis_index("video") * nframes + jnp.arange(rows, dtype=jnp.int32) // POOL
    key_part = lax.all_gather(tkey_flat, "video", axis=0, tiled=True)
    value_part = lax.all_gather(tvalue, "video", axis=0, tiled=True)
    seg_part = lax.all_gather(seg_rows, "video", axis=0, tiled=True)
    count = key_part.shape[0]
    key_frame = jnp.arange(count, dtype=jnp.int32) // POOL
    allowed = (seg_part[None, :] == seg_rows[:, None]) & (
        key_frame[None, :] <= query_frame[:, None]
    )
    logits = (
        jnp.einsum(
            "rhd,khd->hrk",
            tquery,
            key_part.reshape(count, t_heads, HD),
            preferred_element_type=jnp.float32,
        )
        * scale
    )
    weights = jnp.where(allowed[None], jnp.exp(logits), jnp.float32(0.0))
    numer = jnp.einsum(
        "hrk,khd->rhd",
        weights.astype(jnp.bfloat16),
        value_part.reshape(count, t_heads, HD),
        preferred_element_type=jnp.float32,
    )
    denom = jnp.sum(weights, axis=-1)
    numer, denom = (numer, denom)
    summary = numer / jnp.transpose(denom)[:, :, None]
    return summary.reshape(rows, t_heads * HD).astype(jnp.bfloat16)


def solution(mesh):
    return jax.shard_map(
        per_device,
        mesh=mesh,
        in_specs=(
            P(("groups", "video"), None, None),
            P(("groups", "video")),
            P("video", None, "tensor"),
            P("tensor", None, "video"),
        ),
        out_specs=P(("groups", "video"), "tensor"),
        check_vma=False,
    )
```

profile of v0, /device:TPU:0, one launch (start us, length us, event | category | flops | bytes accessed | tf_op | source)
XLA Modules:
  0.0 894.5 jit_solution(1376324522640257826)
XLA Ops:
  6.5 10.3 %copy.32 = bf16[1536,3,768]{0,2,1:T(8,128)(2,1)} copy(bf16[1536,3,768]{2,0,1:T(8,128)(2,1)} %param.6) | data formatting | bytes 14155776 | tf_op args[2]
  16.9 0.7 all-gather.6.cloned.1.call-update
  17.7 5.2 convert_reduce_fusion
  22.9 1.2 copy-done
  24.0 2.6 fusion.2
  26.6 469.2 %all-gather.4.cloned.1.call-done = bf16[6144,3,768]{0,2,1:T(8,128)(2,1)} async-done(((bf16[1536,3,768]{0,2,1:T(8,128)(2,1)}), bf16[6144,3,768]{0,2,1:T(8,128)(2,1)}) %all-gather.4.cloned.1.call-update) | async-done | bytes 28311568 | tf_op jit(solution)/shard_map/all_gather | solution.py:27
  495.8 29.8 %fusion.5 = f32[3,256,3,6,128]{1,4,3,2,0:T(8,128)S(1)} fusion(bf16[3,6,128,6144,1]{3,2,1,0,4:T(8,128)(2,1)} %bitcast.92, bf16[3,256,6144]{2,1,0:T(8,128)(2,1)} %param.4, f32[3,256]{1,0:T(4,128)S(1)} %add_rsqrt_fusion.4, f32[3,256]{1,0:T(4,128)S(1)} %broadcast_multiply_fusion), kind=kOutput, calls=%fused_computation.7 | convolution fusion | flops 21762146304 | bytes 44832768 | tf_op jit(solution)/shard_map/dot_general | solution.py:28
  525.7 0.5 multiply_reduce_fusion.1
  526.2 1.2 fusion.9
  527.4 2.4 fusion.11
  529.7 2.0 copy.36
  531.8 1.0 reduce_sum.86
  533.0 285.3 %all-gather.6.cloned.1.call-done = bf16[768,3,4096]{2,0,1:T(8,128)(2,1)} async-done(((bf16[768,3,1024]{2,0,1:T(8,128)(2,1)}), bf16[768,3,4096]{2,0,1:T(8,128)(2,1)}) %all-gather.6.cloned.1.call-update) | async-done | bytes 18874384 | tf_op jit(solution)/shard_map/all_gather | solution.py:48
  818.2 10.8 %convolution_convert_fusion = bf16[48,3,4096]{2,0,1:T(8,128)(2,1)} fusion(bf16[48,768,1]{1,0,2:T(8,128)(2,1)S(1)} %reshape.178, bf16[768,3,4096]{2,0,1:T(8,128)(2,1)} %all-gather.6.cloned.1.call-done), kind=kOutput, calls=%fused_computation.10 | convolution fusion | flops 906559488 | bytes 20127744 | tf_op jit(solution)/shard_map/rc,ckt->rkt/dot_general | solution.py:45
  829.2 0.6 dynamic-slice
  830.7 7.2 all-reduce
  838.0 15.8 %reduce-scatter.2.cloned.1.call-done = bf16[48,3,1024]{2,0,1:T(8,128)(2,1)} async-done(((bf16[48,3,4096]{2,0,1:T(8,128)(2,1)}), bf16[48,3,1024]{2,0,1:T(8,128)(2,1)}) %reduce-scatter.2.cloned.1.call-update) | async-done | bytes 294928 | tf_op jit(solution)/shard_map/reduce_scatter | solution.py:51
  853.7 0.9 slice.31
  854.6 14.5 %all-gather = bf16[192,1,1024]{2,0,1:T(8,128)(2,1)S(1)} all-gather(bf16[48,1,1024]{2,0,1:T(8,128)(2,1)S(1)} %slice.31), channel_id=2, replica_groups=mesh['groups'=2,'video'=4,'tensor'=4] {'video'}, dimensions={0}, use_global_device_ids=true | all-gather | bytes 491520 | tf_op jit(solution)/shard_map/all_gather | solution.py:62
  869.2 1.0 convert_element_type.61
  871.2 15.4 %all_gather.19 = bf16[192,1024]{1,0:T(8,128)(2,1)S(1)} all-gather(bf16[48,1024]{1,0:T(8,128)(2,1)S(1)} %fusion.25), channel_id=1, replica_groups=mesh['groups'=2,'video'=4,'tensor'=4] {'video'}, dimensions={0}, use_global_device_ids=true | all-gather | bytes 491520 | tf_op jit(solution)/shard_map/all_gather | solution.py:61
  886.6 0.5 fusion.30
  887.1 0.3 fusion.21
  887.3 0.7 copy.70
  (38 shorter events, 1.8 us)
Async XLA Ops:
  6.5 489.3 %all-gather.4.cloned.1.call-start = ((), (), s32[]{:S(2)}) async-start(), calls=%async_computation.1 | async-start | bytes 35389440 | tf_op jit(solution)/shard_map/all_gather | solution.py:27
  16.9 801.4 %all-gather.6.cloned.1.call-start = ((), (), s32[]{:S(2)}) async-start(), calls=%async_computation.2 | async-start | bytes 23592960 | tf_op jit(solution)/shard_map/all_gather | solution.py:48
  17.6 836.1 %reduce-scatter.2.cloned.1.call-start = ((), (), s32[]{:S(2)}) async-start(), calls=%async_computation.3 | async-start | bytes 1474560 | tf_op jit(solution)/shard_map/reduce_scatter | solution.py:51
  17.7 6.4 copy-start
  532.9 296.1 %copy-start.1 = (s32[3]{0:T(128)S(1)}, s32[3]{0:T(128)}, u32[]{:S(2)}) copy-start(s32[3]{0:T(128)} %param.5) | copy-start | bytes 40
  533.0 296.2 %copy-start.2 = (u32[32]{0:T(128)S(1)}, u32[32]{0:T(128)}, u32[]{:S(2)}) copy-start(u32[32]{0:T(128)} %constant.63) | copy-start | bytes 388
Sparse Core Ops, SparseCore 0:
  17.0 478.8 all-gather.3
  497.4 320.7 all-gather.5
  829.2 24.5 reduce-scatter.1
where the time goes:
time: 895 us
  waiting for transfers between devices  771 us (86%)
  matrix products  44.8 us (5%)
  blocking collectives  37.1 us (4%)
  local copies, waits for them, and re-layouts  16.8 us (2%)
  between operations  14 us (2%)
  other arithmetic  10.9 us (1%)
    all_gather x1, waiting for transfers between devices, per_device(): piece = lax.all_gather(qkv_weight, 'video', axis=0, tiled=True)  469 us
    all_gather x1, waiting for transfers between devices, per_device(): lax.all_gather(conn_weight, 'video', axis=2, tiled=True)  285 us
    dot_general x1, matrix products, per_device(): jnp.dot(normed, piece.reshape(piece.shape[0], local_cols), preferred_elem...  29.8 us
  transfers between devices with their start and end apart: 3, of which 3 were waited for; matrix products, arithmetic and copies ran while one was open for 5% of the time, Pallas kernels for 0%

commit v1 on v0

--- a/solution.py
+++ b/solution.py
@@ -58,8 +58,17 @@
     tkey_flat = tkey.reshape(rows, t_heads * HD)
     seg_rows = jnp.repeat(frame_video, POOL)
     query_frame = lax.axis_index("video") * nframes + jnp.arange(rows, dtype=jnp.int32) // POOL
-    key_part = lax.all_gather(tkey_flat, "video", axis=0, tiled=True)
-    value_part = lax.all_gather(tvalue, "video", axis=0, tiled=True)
+
+    def group_sides(local_block, here_x):
+        return jnp.split(
+            lax.all_gather(
+                jnp.concatenate([local_block, here_x], axis=1), "video", axis=0, tiled=True
+            ),
+            [local_block.shape[1]],
+            axis=1,
+        )
+
+    key_part, value_part = group_sides(tkey_flat, tvalue)
     seg_part = lax.all_gather(seg_rows, "video", axis=0, tiled=True)
     count = key_part.shape[0]
     key_frame = jnp.arange(count, dtype=jnp.int32) // POOL

time: 895 us -> 885 us (0.989)
  blocking collectives: 37.1 us -> 26.8 us
    all_gather x2 -> x1, blocking collectives: 29.9 us -> 19.6 us  [group_sides(): lax.all_gather(jnp.concatenate([local_block, here_x], axis=1), 'video', a...]
where the time goes in v1:
time: 885 us; the launch traced here: 884 us
  waiting for transfers between devices  771 us (87%)
  matrix products  44.8 us (5%)
  blocking collectives  26.8 us (3%)
  local copies, waits for them, and re-layouts  16.8 us (2%)
  between operations  14 us (2%)
  other arithmetic  10.9 us (1%)
    all_gather x1, waiting for transfers between devices, per_device(): piece = lax.all_gather(qkv_weight, 'video', axis=0, tiled=True)  469 us
    all_gather x1, waiting for transfers between devices, per_device(): lax.all_gather(conn_weight, 'video', axis=2, tiled=True)  285 us
    dot_general x1, matrix products, per_device(): jnp.dot(normed, piece.reshape(piece.shape[0], local_cols), preferred_elem...  29.8 us
    all_gather x1, blocking collectives, group_sides(): lax.all_gather(jnp.concatenate([local_block, here_x], axis=1), 'video', a...  19.6 us
  transfers between devices with their start and end apart: 3, of which 3 were waited for; matrix products, arithmetic and copies ran while one was open for 5% of the time, Pallas kernels for 0%

profile of v1, /device:TPU:0, one launch (start us, length us, event | category | flops | bytes accessed | tf_op | source)
XLA Modules:
  0.0 884.2 jit_solution(17778950524951157956)
XLA Ops:
  6.5 10.3 %copy.32 = bf16[1536,3,768]{0,2,1:T(8,128)(2,1)} copy(bf16[1536,3,768]{2,0,1:T(8,128)(2,1)} %param.6) | data formatting | bytes 14155776 | tf_op args[2]
  16.9 0.7 all-gather.5.cloned.1.call-update
  17.7 5.2 convert_reduce_fusion
  22.9 1.2 copy-done
  24.0 2.6 fusion.2
  26.6 469.2 %all-gather.3.cloned.1.call-done = bf16[6144,3,768]{0,2,1:T(8,128)(2,1)} async-done(((bf16[1536,3,768]{0,2,1:T(8,128)(2,1)}), bf16[6144,3,768]{0,2,1:T(8,128)(2,1)}) %all-gather.3.cloned.1.call-update) | async-done | bytes 28311568 | tf_op jit(solution)/shard_map/all_gather | solution.py:27
  495.8 29.8 %fusion.5 = f32[3,256,3,6,128]{1,4,3,2,0:T(8,128)S(1)} fusion(bf16[3,6,128,6144,1]{3,2,1,0,4:T(8,128)(2,1)} %bitcast.91, bf16[3,256,6144]{2,1,0:T(8,128)(2,1)} %param.4, f32[3,256]{1,0:T(4,128)S(1)} %add_rsqrt_fusion.4, f32[3,256]{1,0:T(4,128)S(1)} %broadcast_multiply_fusion), kind=kOutput, calls=%fused_computation.7 | convolution fusion | flops 21762146304 | bytes 44832768 | tf_op jit(solution)/shard_map/dot_general | solution.py:28
  525.7 0.5 multiply_reduce_fusion.1
  526.2 1.2 fusion.9
  527.4 2.4 fusion.11
  529.7 2.0 copy.36
  531.8 1.0 reduce_sum.86
  533.0 285.3 %all-gather.5.cloned.1.call-done = bf16[768,3,4096]{2,0,1:T(8,128)(2,1)} async-done(((bf16[768,3,1024]{2,0,1:T(8,128)(2,1)}), bf16[768,3,4096]{2,0,1:T(8,128)(2,1)}) %all-gather.5.cloned.1.call-update) | async-done | bytes 18874384 | tf_op jit(solution)/shard_map/all_gather | solution.py:48
  818.2 10.8 %convolution_convert_fusion = bf16[48,3,4096]{2,0,1:T(8,128)(2,1)} fusion(bf16[48,768,1]{1,0,2:T(8,128)(2,1)S(1)} %reshape.176, bf16[768,3,4096]{2,0,1:T(8,128)(2,1)} %all-gather.5.cloned.1.call-done), kind=kOutput, calls=%fused_computation.10 | convolution fusion | flops 906559488 | bytes 20127744 | tf_op jit(solution)/shard_map/rc,ckt->rkt/dot_general | solution.py:45
  829.2 0.6 dynamic-slice
  830.5 0.2 dynamic-update-slice
  830.7 7.2 all-reduce
  838.0 15.8 %reduce-scatter.2.cloned.1.call-done = bf16[48,3,1024]{2,0,1:T(8,128)(2,1)} async-done(((bf16[48,3,4096]{2,0,1:T(8,128)(2,1)}), bf16[48,3,1024]{2,0,1:T(8,128)(2,1)}) %reduce-scatter.2.cloned.1.call-update) | async-done | bytes 294928 | tf_op jit(solution)/shard_map/reduce_scatter | solution.py:51
  853.7 1.0 convert_element_type.60
  855.3 0.9 slice_bitcast_fusion.5
  856.2 19.6 %all_gather.14 = bf16[192,2048]{1,0:T(8,128)(2,1)S(1)} all-gather(bf16[48,2048]{1,0:T(8,128)(2,1)S(1)} %pad_maximum_fusion), channel_id=1, replica_groups=mesh['groups'=2,'video'=4,'tensor'=4] {'video'}, dimensions={0}, use_global_device_ids=true | all-gather | bytes 983040 | tf_op jit(solution)/shard_map/all_gather | solution.py:64
  876.3 0.5 fusion.31
  876.8 0.3 fusion.21
  877.0 0.7 copy.72
  (38 shorter events, 1.6 us)
Async XLA Ops:
  6.5 489.3 %all-gather.3.cloned.1.call-start = ((), (), s32[]{:S(2)}) async-start(), calls=%async_computation.1 | async-start | bytes 35389440 | tf_op jit(solution)/shard_map/all_gather | solution.py:27
  16.9 801.4 %all-gather.5.cloned.1.call-start = ((), (), s32[]{:S(2)}) async-start(), calls=%async_computation.2 | async-start | bytes 23592960 | tf_op jit(solution)/shard_map/all_gather | solution.py:48
  17.6 836.1 %reduce-scatter.2.cloned.1.call-start = ((), (), s32[]{:S(2)}) async-start(), calls=%async_computation.3 | async-start | bytes 1474560 | tf_op jit(solution)/shard_map/reduce_scatter | solution.py:51
  17.7 6.4 copy-start
  532.9 296.1 %copy-start.1 = (s32[3]{0:T(128)S(1)}, s32[3]{0:T(128)}, u32[]{:S(2)}) copy-start(s32[3]{0:T(128)} %param.5) | copy-start | bytes 40
  533.0 296.2 %copy-start.2 = (u32[32]{0:T(128)S(1)}, u32[32]{0:T(128)}, u32[]{:S(2)}) copy-start(u32[32]{0:T(128)} %constant.63) | copy-start | bytes 388
Sparse Core Ops, SparseCore 0:
  17.0 478.8 all-gather.2
  497.4 320.7 all-gather.4
  829.2 24.5 reduce-scatter.1
